TPU v7x, 512 devices: a whole 4x8x8 slice. The times are simulated.
512 devices in a mesh: col: 32 (over x_lo, z, core), rec: 16 (over x_hi, y).
Axes of the slice: x: 4 (x_hi: 2, x_lo: 2; x = x_hi * 2 + x_lo), y: 8, z: 8, core: 2. Of those that a mesh axis runs over, the one named last changes fastest.
Arguments:
- design: bfloat16 [4096, 16384], P('rec', 'col')
- record_weight: float32 [4096], P('rec'), may hold values from 0.5 to 3.47
Outputs:
- rotated_design: bfloat16 [4096, 16384], P('rec', 'col')
- column_rms: float32 [16384], P('col')
All inputs are finite; a program needn't handle non-finite values.
Results may differ from a plain program's by a relative error of at most 0.0088.
Values may be sent and summed in bfloat16 or wider, within the bound.
No kernel may reach another device: no remote copies, remote signals or barrier semaphores. Data moves between devices by JAX's collectives and lax.ppermute only.
A program may use at most 64 MiB of HBM per device.

v0:
```python
import jax
import jax.numpy as jnp
from jax import lax
from jax.sharding import PartitionSpec as P

ROUNDS = 3
SWEEPS = 6
eps_angle = 0.01


def from_behind(value, axis, steps):
    count = lax.axis_size(axis)
    leading, last = (max(0, -steps), min(count, count - steps))
    return lax.ppermute(value, axis, [(source, source + steps) for source in range(leading, last)])


def jacobi_sweeps(gram_matrix, width):
    top_left = gram_matrix[:width, :width]
    top_right = gram_matrix[:width, width:]
    low_left = gram_matrix[width:, :width]
    low_right = gram_matrix[width:, width:]
    identity = jnp.eye(2 * width, dtype=jnp.float32)
    rot_first = identity[:, :width]
    rot_second = identity[:, width:]
    for sweep_index in range(SWEEPS):
        if sweep_index > 0:
            top_right = jnp.roll(top_right, -1, axis=1)
            low_left = jnp.roll(low_left, -1, axis=0)
            low_right = jnp.roll(jnp.roll(low_right, -1, axis=0), -1, axis=1)
            rot_second = jnp.roll(rot_second, -1, axis=1)
        first_diag = jnp.diagonal(top_left)
        second_diag = jnp.diagonal(low_right)
        coupling = jnp.diagonal(top_right)
        spread = second_diag - first_diag
        tangent = (
            2.0
            * coupling
            * spread
            / (
                spread * spread
                + 4.0 * coupling * coupling
                + eps_angle * (first_diag + second_diag) ** 2
            )
        )
        half_angle = 0.5 * jnp.arctan(tangent)
        cosine = jnp.cos(half_angle)
        sine_value = jnp.sin(half_angle)
        cos_col = cosine[None, :]
        sin_col = sine_value[None, :]
        cos_row = cosine[:, None]
        sin_row = sine_value[:, None]
        left_a = top_left * cos_col - top_right * sin_col
        right_a = top_left * sin_col + top_right * cos_col
        left_b = low_left * cos_col - low_right * sin_col
        right_b = low_left * sin_col + low_right * cos_col
        top_left = cos_row * left_a - sin_row * left_b
        low_left = sin_row * left_a + cos_row * left_b
        top_right = cos_row * right_a - sin_row * right_b
        low_right = sin_row * right_a + cos_row * right_b
        rot_first, rot_second = (
            rot_first * cos_col - rot_second * sin_col,
            rot_first * sin_col + rot_second * cos_col,
        )
    rot_second = jnp.roll(rot_second, SWEEPS - 1, axis=1)
    return jnp.concatenate([rot_first, rot_second], axis=1)


def send_right(block):
    return from_behind(block, "col", 1)


def send_left(block):
    return from_behind(block, "col", -1)


def inner_products(left_part, right_part):
    return lax.dot_general(
        left_part, right_part, (((0,), (0,)), ((), ())), preferred_element_type=jnp.float32
    )


def local(design, record_weight):
    width = design.shape[1] // 2
    weighted = (design.astype(jnp.float32) * record_weight[:, None]).astype(jnp.bfloat16)
    upper_block = weighted[:, :width]
    lower_block = weighted[:, width:]
    position = lax.axis_index("col")
    device_count = lax.axis_size("col")
    for round_index in range(ROUNDS):
        moving = round_index + 1 < ROUNDS
        pair_data = jnp.concatenate([upper_block, lower_block], axis=1)
        gram_matrix = lax.psum(inner_products(pair_data, pair_data), "rec")
        rotation = jacobi_sweeps(gram_matrix, width).astype(jnp.bfloat16)
        rotated = jnp.dot(pair_data, rotation, preferred_element_type=jnp.float32).astype(
            jnp.bfloat16
        )
        new_upper = rotated[:, :width]
        new_lower = rotated[:, width:]
        if moving:
            from_right = send_left(new_lower)
            from_left = send_right(jnp.where(position == 0, new_lower, new_upper))
        if moving:
            upper_block = jnp.where(position == 0, new_upper, from_left)
            lower_block = jnp.where(position == device_count - 1, new_upper, from_right)
        else:
            upper_block = new_upper
            lower_block = new_lower
    rotated_design = jnp.concatenate([upper_block, lower_block], axis=1)
    squares = jnp.sum(jnp.square(rotated_design.astype(jnp.float32)), axis=0)
    totals = lax.psum(squares, "rec")
    record_total = design.shape[0] * lax.axis_size("rec")
    column_rms = jnp.sqrt(totals / record_total + 1e-06)
    return (rotated_design, column_rms)


def solution(mesh):
    placed = (P("rec", "col"), P("rec"))
    return jax.shard_map(
        local, mesh=mesh, in_specs=placed, out_specs=(P("rec", "col"), P("col")), check_vma=False
    )
```

profile of v0, /device:TPU:64, one launch (start us, length us, event | category | flops | bytes accessed | tf_op | source)
XLA Modules:
  0.0 738.1 jit_solution(11142493049382048583)
XLA Ops:
  7.2 2.5 fusion.33
  9.9 168.6 %all-reduce.4.cloned.1.call-done = f32[512,512]{1,0:T(8,128)} async-done(((f32[512,512]{1,0:T(8,128)}), f32[512,512]{1,0:T(8,128)}) %all-reduce.4.cloned.1.call-update) | async-done | bytes 1048592 | tf_op jit(solution)/shard_map/psum | solution.py:92
  179.6 2.3 gather_fusion
  182.0 2.3 gather_fusion.2
  184.3 2.3 gather_fusion.1
  187.3 2.3 gather_fusion.5
  189.9 2.3 gather_fusion.4
  192.3 2.3 gather_fusion.3
  195.2 2.3 gather_fusion.8
  197.7 2.3 gather_fusion.6
  200.3 2.3 gather_fusion.7
  203.3 2.3 gather_fusion.11
  205.7 2.3 gather_fusion.9
  208.3 2.3 gather_fusion.10
  211.3 2.3 gather_fusion.14
  213.8 2.3 gather_fusion.12
  216.4 2.5 gather_fusion.13
  223.2 2.9 gather_fusion.17
  227.2 2.3 gather_fusion.15
  229.9 2.3 gather_fusion.16
  234.0 1.9 collective-permute-start
  236.0 3.6 collective-permute-start.1
  240.3 1.8 collective-permute-done.1
  243.5 162.9 %all-reduce.6.cloned.1.call-done = f32[512,512]{1,0:T(8,128)} async-done(((f32[512,512]{1,0:T(8,128)}), f32[512,512]{1,0:T(8,128)}) %all-reduce.6.cloned.1.call-update) | async-done | bytes 1048592 | tf_op jit(solution)/shard_map/psum | solution.py:92
  407.6 2.3 gather_fusion.18
  410.0 2.3 gather_fusion.20
  412.3 2.3 gather_fusion.19
  415.3 2.3 gather_fusion.23
  417.8 2.3 gather_fusion.21
  420.4 2.3 gather_fusion.22
  423.3 2.3 gather_fusion.26
  425.8 2.3 gather_fusion.24
  428.4 2.3 gather_fusion.25
  431.4 2.3 gather_fusion.29
  433.9 2.3 gather_fusion.27
  436.5 2.3 gather_fusion.28
  439.5 2.3 gather_fusion.32
  441.9 2.3 gather_fusion.30
  444.5 2.6 gather_fusion.31
  452.1 2.9 gather_fusion.35
  456.1 2.9 gather_fusion.33
  459.3 2.9 gather_fusion.34
  464.7 1.9 collective-permute-start.2
  466.6 3.6 collective-permute-start.3
  474.1 163.0 %all-reduce.8.cloned.1.call-done = f32[512,512]{1,0:T(8,128)} async-done(((f32[512,512]{1,0:T(8,128)}), f32[512,512]{1,0:T(8,128)}) %all-reduce.8.cloned.1.call-update) | async-done | bytes 1048592 | tf_op jit(solution)/shard_map/psum | solution.py:92
  638.3 2.3 gather_fusion.36
  640.7 2.3 gather_fusion.38
  643.0 2.3 gather_fusion.37
  646.0 2.3 gather_fusion.41
  648.4 2.3 gather_fusion.39
  651.0 2.3 gather_fusion.40
  654.0 2.3 gather_fusion.44
  656.5 2.3 gather_fusion.42
  659.1 2.3 gather_fusion.43
  662.1 2.3 gather_fusion.47
  664.6 2.3 gather_fusion.45
  667.2 2.3 gather_fusion.46
  670.1 2.3 gather_fusion.50
  672.6 2.3 gather_fusion.48
  675.2 2.6 gather_fusion.49
  680.7 2.3 gather_fusion.53
  683.2 2.3 gather_fusion.51
  685.8 2.3 gather_fusion.52
  689.8 40.8 %psum.31 = f32[512]{0:T(512)S(1)} all-reduce(f32[512]{0:T(512)S(1)} %get-tuple-element.130), channel_id=1, replica_groups=mesh['col'=32,'rec'=16] {'rec'}, use_global_device_ids=true, to_apply=%region_4.5 | all-reduce | flops 512 | bytes 4096 | tf_op jit(solution)/shard_map/psum | solution.py:110
  (276 shorter events, 41.5 us)
Async XLA Ops:
  7.2 171.3 %all-reduce.4.cloned.1.call-start = ((), (), s32[]{:S(2)}) async-start(), calls=%async_computation | async-start | bytes 2097152 | tf_op jit(solution)/shard_map/psum | solution.py:92
  9.7 396.8 %all-reduce.6.cloned.1.call-start = ((), (), s32[]{:S(2)}) async-start(), calls=%async_computation.1 | async-start | bytes 2097152 | tf_op jit(solution)/shard_map/psum | solution.py:92
  182.0 4.8 copy-start
  229.8 2.4 copy-start.8
  229.8 2.5 copy-start.3
  232.7 1.0 copy-start.7
  232.8 0.8 copy-start.10
  234.0 6.3 collective-permute-start
  236.0 6.1 collective-permute-start.1
  242.1 1.3 copy-start.5
  243.5 393.7 %all-reduce.8.cloned.1.call-start = ((), (), s32[]{:S(2)}) async-start(), calls=%async_computation.2 | async-start | bytes 2097152 | tf_op jit(solution)/shard_map/psum | solution.py:92
  410.0 4.8 copy-start.1
  459.3 3.0 copy-start.9
  459.3 3.8 copy-start.4
  463.4 0.9 copy-start.6
  464.7 6.3 collective-permute-start.2
  466.6 6.1 collective-permute-start.3
  640.6 4.8 copy-start.2
Sparse Core Ops, SparseCore 0:
  10.9 167.4 all-reduce.3
  243.6 162.8 all-reduce.5
  474.2 162.8 all-reduce.7
where the time goes:
time: 746 us; the launch traced here: 738 us
  waiting for transfers between devices  500 us (67%)
  local copies, waits for them, and re-layouts  145 us (19%)
  blocking collectives  40.8 us (5%)
  other arithmetic  18.2 us (2%)
  between operations  16.3 us (2%)
  starting transfers between devices  11.2 us (2%)
    psum x3, waiting for transfers between devices, local(): gram_matrix = lax.psum(inner_products(pair_data, pair_data), 'rec')  495 us
    gather x18, local copies, waits for them, and re-layouts, jacobi_sweeps(): second_diag = jnp.diagonal(low_right)  43.4 us
    gather x18, local copies, waits for them, and re-layouts, jacobi_sweeps(): first_diag = jnp.diagonal(top_left)  43.4 us
    gather x18, local copies, waits for them, and re-layouts, jacobi_sweeps(): coupling = jnp.diagonal(top_right)  42.8 us
    psum x1, blocking collectives, local(): totals = lax.psum(squares, 'rec')  40.8 us
  transfers between devices with their start and end apart: 7, of which 7 were waited for; matrix products, arithmetic and copies ran while one was open for 0% of the time, Pallas kernels for 0%

commit v1 on v0

--- a/solution.py
+++ b/solution.py
@@ -89,7 +89,7 @@
     for round_index in range(ROUNDS):
         moving = round_index + 1 < ROUNDS
         pair_data = jnp.concatenate([upper_block, lower_block], axis=1)
-        gram_matrix = lax.psum(inner_products(pair_data, pair_data), "rec")
+        gram_matrix = jnp.sum(lax.all_gather(inner_products(pair_data, pair_data), "rec"), axis=0)
         rotation = jacobi_sweeps(gram_matrix, width).astype(jnp.bfloat16)
         rotated = jnp.dot(pair_data, rotation, preferred_element_type=jnp.float32).astype(
             jnp.bfloat16

time: 746 us -> 963 us (1.29)
  the two profiles are of different devices: /device:TPU:64 before, /device:TPU:2 now
where the time goes in v1:
time: 963 us; the launch traced here: 960 us
  waiting for transfers between devices  694 us (72%)
  local copies, waits for them, and re-layouts  141 us (15%)
  other arithmetic  45.3 us (5%)
  blocking collectives  38.9 us (4%)
  between operations  16 us (2%)
  starting transfers between devices  15.5 us (2%)
    all_gather x3, waiting for transfers between devices, local(): lax.all_gather(inner_products(pair_data, pair_data), 'rec')  689 us
    gather x18, local copies, waits for them, and re-layouts, jacobi_sweeps(): coupling = jnp.diagonal(top_right)  44 us
    gather x18, local copies, waits for them, and re-layouts, jacobi_sweeps(): first_diag = jnp.diagonal(top_left)  44 us
    gather x18, local copies, waits for them, and re-layouts, jacobi_sweeps(): second_diag = jnp.diagonal(low_right)  42.8 us
    psum x1, blocking collectives, local(): totals = lax.psum(squares, 'rec')  38.9 us
    reduce_sum x3, other arithmetic, local(): jnp.sum(lax.all_gather(inner_products(pair_data, pair_data), 'rec'), axis=0)  23.9 us
  transfers between devices with their start and end apart: 7, of which 7 were waited for; matrix products, arithmetic and copies ran while one was open for 0% of the time, Pallas kernels for 0%

profile of v1, /device:TPU:2, one launch (start us, length us, event | category | flops | bytes accessed | tf_op | source)
XLA Modules:
  0.0 960.2 jit_solution(9625380921237258657)
XLA Ops:
  7.2 2.5 fusion.33
  9.9 235.2 %all-gather.7.cloned.1.call-done = f32[8192,512]{1,0:T(8,128)} async-done(((f32[512,512]{1,0:T(8,128)}), f32[8192,512]{1,0:T(8,128)}) %all-gather.7.cloned.1.call-update) | async-done | bytes 16777232 | tf_op jit(solution)/shard_map/all_gather | solution.py:92
  245.1 8.0 reduce_sum.36
  253.1 2.9 gather_fusion
  256.0 2.3 gather_fusion.2
  258.4 2.3 gather_fusion.1
  261.3 2.3 gather_fusion.5
  264.0 2.3 gather_fusion.4
  266.3 2.3 gather_fusion.3
  269.3 2.3 gather_fusion.8
  271.7 2.3 gather_fusion.6
  274.3 2.3 gather_fusion.7
  277.3 2.3 gather_fusion.11
  279.8 2.3 gather_fusion.9
  282.4 2.3 gather_fusion.10
  285.4 2.3 gather_fusion.14
  287.8 2.3 gather_fusion.12
  290.4 2.5 gather_fusion.13
  297.3 2.9 gather_fusion.17
  301.3 2.3 gather_fusion.15
  303.9 2.3 gather_fusion.16
  311.7 5.8 collective-permute-start.1
  321.4 227.0 %all-gather.9.cloned.1.call-done = f32[8192,512]{1,0:T(8,128)} async-done(((f32[512,512]{1,0:T(8,128)}), f32[8192,512]{1,0:T(8,128)}) %all-gather.9.cloned.1.call-update) | async-done | bytes 16777232 | tf_op jit(solution)/shard_map/all_gather | solution.py:92
  548.4 8.0 reduce_sum.37
  556.4 2.6 gather_fusion.18
  559.0 2.3 gather_fusion.20
  561.4 2.3 gather_fusion.19
  564.3 2.3 gather_fusion.23
  566.8 2.3 gather_fusion.21
  569.4 2.3 gather_fusion.22
  572.4 2.3 gather_fusion.26
  574.8 2.3 gather_fusion.24
  577.4 2.3 gather_fusion.25
  580.4 2.3 gather_fusion.29
  582.9 2.3 gather_fusion.27
  585.5 2.3 gather_fusion.28
  588.5 2.3 gather_fusion.32
  591.0 2.3 gather_fusion.30
  593.6 2.6 gather_fusion.31
  601.1 2.9 gather_fusion.35
  605.2 2.9 gather_fusion.33
  608.4 2.3 gather_fusion.34
  616.1 5.8 collective-permute-start.3
  625.7 227.1 %all-gather.11.cloned.1.call-done = f32[8192,512]{1,0:T(8,128)} async-done(((f32[512,512]{1,0:T(8,128)}), f32[8192,512]{1,0:T(8,128)}) %all-gather.11.cloned.1.call-update) | async-done | bytes 16777232 | tf_op jit(solution)/shard_map/all_gather | solution.py:92
  852.8 8.0 reduce_sum.38
  860.8 2.8 gather_fusion.36
  863.7 2.3 gather_fusion.38
  866.0 2.3 gather_fusion.37
  869.0 2.3 gather_fusion.41
  871.4 2.3 gather_fusion.39
  874.0 2.3 gather_fusion.40
  877.0 2.3 gather_fusion.44
  879.5 2.3 gather_fusion.42
  882.1 2.3 gather_fusion.43
  885.1 2.3 gather_fusion.47
  887.5 2.3 gather_fusion.45
  890.2 2.3 gather_fusion.46
  893.1 2.3 gather_fusion.50
  895.6 2.3 gather_fusion.48
  898.2 2.5 gather_fusion.49
  903.7 2.9 gather_fusion.53
  906.7 2.3 gather_fusion.51
  909.3 2.3 gather_fusion.52
  913.9 38.9 %psum.7 = f32[512]{0:T(512)S(1)} all-reduce(f32[512]{0:T(512)S(1)} %get-tuple-element.130), channel_id=1, replica_groups=mesh['col'=32,'rec'=16] {'rec'}, use_global_device_ids=true, to_apply=%region_4.5 | all-reduce | flops 512 | bytes 4096 | tf_op jit(solution)/shard_map/psum | solution.py:110
  (259 shorter events, 47.4 us)
Async XLA Ops:
  7.2 237.9 %all-gather.7.cloned.1.call-start = ((), (), s32[]{:S(2)}) async-start(), calls=%async_computation | async-start | bytes 17825792 | tf_op jit(solution)/shard_map/all_gather | solution.py:92
  9.7 538.7 %all-gather.9.cloned.1.call-start = ((), (), s32[]{:S(2)}) async-start(), calls=%async_computation.1 | async-start | bytes 17825792 | tf_op jit(solution)/shard_map/all_gather | solution.py:92
  309.8 8.4 collective-permute-start
  311.7 8.3 collective-permute-start.1
  320.0 228.4 %copy-start = (bf16[256,256]{1,0:T(8,128)(2,1)}, bf16[256,256]{1,0:T(8,128)(2,1)S(1)}, u32[]{:S(2)}) copy-start(bf16[256,256]{1,0:T(8,128)(2,1)S(1)} %get-tuple-element.127) | copy-start | bytes 393220
  321.3 531.5 %all-gather.11.cloned.1.call-start = ((), (), s32[]{:S(2)}) async-start(), calls=%async_computation.2 | async-start | bytes 17825792 | tf_op jit(solution)/shard_map/all_gather | solution.py:92
  614.2 8.4 collective-permute-start.2
  616.1 8.3 collective-permute-start.3
Sparse Core Ops, SparseCore 0:
  11.2 233.8 all-gather.6
  321.5 226.9 all-gather.8
  625.9 226.9 all-gather.10
